TPU v7x, 32 devices: a whole 2x2x4 slice. The times are simulated.
32 devices in a mesh: ctx: 8 (over z, y), dp: 2 (over x), section: 2 (over core).
Axes of the slice: x: 2, y: 2, z: 4, core: 2. Of those that a mesh axis runs over, the one named last changes fastest.
Arguments:
- normed: bfloat16 [2, 3072, 1024], P('dp', 'ctx'), may hold values from -40 to 40
- w_query: bfloat16 [1024, 1024], P('dp', 'section'), may hold values from -0.1875 to 0.1875
- w_key: bfloat16 [1024, 1024], P('dp', 'section'), may hold values from -0.28125 to 0.28125
- w_value: bfloat16 [1024, 1024], P('dp', 'section'), may hold values from -0.1875 to 0.1875
- block_mask: int32 [24, 7], replicated, may hold values from 0 to 1, as said below
- cotangent: bfloat16 [2, 3072, 1024], P('dp', 'ctx', 'section'), may hold values from -8 to 8
Outputs:
- attended: bfloat16 [2, 3072, 1024], P('dp', 'ctx', 'section')
- grad_input: bfloat16 [2, 3072, 1024], P('dp', 'ctx')
- grad_weights: float32 [1024, 3, 1024], P(('ctx', 'dp'), None, 'section')
Inputs may be any that keep to these rules, and one draw needn't show every extreme that they name: `block_mask`: every row has a 1 in column 3; no row names a key block outside 0 to 23; a row holds at most 5 ones, and some row holds exactly 5.
All inputs are finite; a program needn't handle non-finite values.
Results may differ from a plain program's by a relative error of at most 0.014.
The roundings to bfloat16 on the way count: a program that leaves them out, or rounds other values in their place, can miss the bound.
Values may be sent and summed in bfloat16 or wider, within the bound.
No kernel may reach another device: no remote copies, remote signals or barrier semaphores. Data moves between devices by JAX's collectives and lax.ppermute only.
A program may use at most 64 MiB of HBM per device.

v0:
```python
import jax
import jax.numpy as jnp
from jax import lax
from jax.sharding import PartitionSpec as P

HD = 64
BLOCK = 128
REACH = 3


def extended(cells, sides, width):
    for axis, dim in sides:
        count = lax.axis_size(axis)
        ends = count - 1
        head = lax.slice_in_dim(cells, 0, width, axis=dim)
        tail = lax.slice_in_dim(cells, cells.shape[dim] - width, cells.shape[dim], axis=dim)
        cells = jnp.concatenate(
            [
                lax.ppermute(tail, axis, [(i, (i + 1) % count) for i in range(ends)]),
                cells,
                lax.ppermute(head, axis, [((i + 1) % count, i) for i in range(ends)]),
            ],
            axis=dim,
        )
    return cells


def shifted(value, axis, steps):
    count = lax.axis_size(axis)
    leading, last = (max(0, -steps), min(count, count - steps))
    return lax.ppermute(value, axis, [(source, source + steps) for source in range(leading, last)])


def attend(query_block, key_window, seen_slots, score_scale):
    scores = (
        jnp.einsum("qhd,skhd->hqsk", query_block, key_window, preferred_element_type=jnp.float32)
        * score_scale
    )
    is_seen = seen_slots[None, None, :, None] > 0
    row_top = jnp.max(jnp.where(is_seen, scores, -jnp.inf), axis=(2, 3), keepdims=True)
    raised = jnp.where(is_seen, jnp.exp(scores - row_top), 0.0)
    row_total = jnp.sum(raised, axis=(2, 3), keepdims=True)
    return (raised / row_total, row_top, row_total)


def per_device(normed, w_query, w_key, w_value, block_mask, cotangent):
    tokens = normed[0]
    upstream = cotangent[0]
    length = tokens.shape[0]
    features = upstream.shape[1]
    head_count = features // HD
    blocks = length // BLOCK
    frame_len = blocks + 2 * REACH
    span_len = 2 * REACH + 1
    score_scale = HD ** (-0.5)
    query_full, key_full, value_full = (
        lax.all_gather(w_query, "dp", axis=0, tiled=True),
        lax.all_gather(w_key, "dp", axis=0, tiled=True),
        lax.all_gather(w_value, "dp", axis=0, tiled=True),
    )
    queries = jnp.dot(tokens, query_full, preferred_element_type=jnp.float32).astype(jnp.bfloat16)
    key_rows = jnp.dot(tokens, key_full, preferred_element_type=jnp.float32).astype(jnp.bfloat16)
    value_rows = jnp.dot(tokens, value_full, preferred_element_type=jnp.float32).astype(
        jnp.bfloat16
    )
    framed = extended(jnp.stack([key_rows, value_rows]), (("ctx", 1),), REACH * BLOCK)
    framed = framed.reshape(2, frame_len, BLOCK, head_count, HD)
    query_blocks = queries.reshape(blocks, BLOCK, head_count, HD)
    upstream_blocks = upstream.reshape(blocks, BLOCK, head_count, HD)
    first_block = lax.axis_index("ctx") * blocks
    padded_mask = jnp.pad(block_mask, ((REACH, REACH), (0, 0)))
    frame_mask = lax.dynamic_slice(padded_mask, (first_block, 0), (frame_len, span_len))
    own_mask = frame_mask[REACH : REACH + blocks]
    positions = jnp.arange(span_len, dtype=jnp.int32)
    slot_order = jnp.broadcast_to(positions[None, :], (blocks, span_len))
    slot_index = slot_order + jnp.arange(blocks, dtype=jnp.int32)[:, None]

    def windows(block_at):
        picked = lax.dynamic_slice_in_dim(framed, block_at, span_len, 1)
        return (picked[0], picked[1])

    def forward(running, block_at):
        query_block = lax.dynamic_index_in_dim(query_blocks, block_at, 0, False)
        key_window, value_window = windows(block_at)
        seen_slots = lax.dynamic_index_in_dim(own_mask, block_at, 0, False)
        probability, row_top, row_total = attend(query_block, key_window, seen_slots, score_scale)
        mixed_out = jnp.einsum(
            "hqsk,skhd->qhd",
            probability.astype(jnp.bfloat16),
            value_window,
            preferred_element_type=jnp.float32,
        ).astype(jnp.bfloat16)
        return (running, (mixed_out, row_top[:, :, 0, 0], row_total[:, :, 0, 0]))

    block_ids = jnp.arange(blocks, dtype=jnp.int32)
    _, (mixed_outs, row_tops, row_totals) = lax.scan(forward, jnp.zeros((), jnp.float32), block_ids)
    attended = mixed_outs.reshape(1, length, features)

    def backward(running, block_at):
        query_block = lax.dynamic_index_in_dim(query_blocks, block_at, 0, False)
        upstream_block = lax.dynamic_index_in_dim(upstream_blocks, block_at, 0, False)
        key_window, value_window = windows(block_at)
        seen_slots = lax.dynamic_index_in_dim(own_mask, block_at, 0, False)
        probability, _, _ = attend(query_block, key_window, seen_slots, score_scale)
        weights = probability.astype(jnp.bfloat16)
        prob_grad = jnp.einsum(
            "qhd,skhd->hqsk", upstream_block, value_window, preferred_element_type=jnp.float32
        )
        row_delta = jnp.sum(probability * prob_grad, axis=(2, 3), keepdims=True)
        score_grad = (probability * (prob_grad - row_delta)).astype(jnp.bfloat16)
        query_grad = (
            score_scale
            * jnp.einsum(
                "hqsk,skhd->qhd", score_grad, key_window, preferred_element_type=jnp.float32
            )
        ).astype(jnp.bfloat16)
        key_part = score_scale * jnp.einsum(
            "hqsk,qhd->skhd", score_grad, query_block, preferred_element_type=jnp.float32
        )
        value_part = jnp.einsum(
            "hqsk,qhd->skhd", weights, upstream_block, preferred_element_type=jnp.float32
        )
        slot_rows = lax.dynamic_index_in_dim(slot_index, block_at, 0, False)
        running = running.at[0, slot_rows].add(key_part).at[1, slot_rows].add(value_part)
        return (running, (query_grad, row_delta[:, :, 0, 0]))

    start_state = jnp.zeros((2, frame_len, BLOCK, head_count, HD), jnp.float32)
    frame_grads, (query_grads, row_deltas) = lax.scan(backward, start_state, block_ids)
    query_grad = query_grads.reshape(length, features)
    frame_grads = frame_grads.reshape(2, frame_len, BLOCK, features)
    left_side = frame_grads[:, :REACH]
    right_side = frame_grads[:, blocks + REACH :]
    middle = frame_grads[:, REACH : REACH + blocks]
    for offset in (1, -1):
        outgoing = right_side if offset == 1 else left_side
        arrived = shifted(outgoing.astype(jnp.bfloat16), "ctx", offset).astype(outgoing.dtype)
        if offset == 1:
            middle = middle.at[:, :REACH].add(arrived)
        else:
            middle = middle.at[:, blocks - REACH :].add(arrived)
    key_grad = middle[0].reshape(length, features).astype(jnp.bfloat16)
    value_grad = middle[1].reshape(length, features).astype(jnp.bfloat16)
    contract = (((1,), (1,)), ((), ()))
    partial_input = (
        lax.dot_general(query_grad, query_full, contract, preferred_element_type=jnp.float32)
        + lax.dot_general(key_grad, key_full, contract, preferred_element_type=jnp.float32)
        + lax.dot_general(value_grad, value_full, contract, preferred_element_type=jnp.float32)
    )
    grad_input = lax.psum(partial_input.astype(jnp.bfloat16), "section")[None]
    grads_all = jnp.stack([query_grad, key_grad, value_grad], axis=1)
    group_part = lax.psum_scatter(
        jnp.einsum("tr,tcf->rcf", tokens, grads_all, preferred_element_type=jnp.float32).astype(
            jnp.bfloat16
        ),
        "ctx",
        scatter_dimension=0,
        tiled=True,
    )
    summed = lax.psum_scatter(group_part, "dp", scatter_dimension=0, tiled=True).astype(jnp.float32)
    grad_weights = summed / lax.axis_size("dp")
    return (attended, grad_input, grad_weights)


def solution(mesh):
    in_specs = (
        P("dp", "ctx", None),
        P("dp", "section"),
        P("dp", "section"),
        P("dp", "section"),
        P(),
        P("dp", "ctx", "section"),
    )
    out_specs = (P("dp", "ctx", "section"), P("dp", "ctx", None), P(("ctx", "dp"), None, "section"))
    return jax.shard_map(
        per_device, mesh=mesh, in_specs=in_specs, out_specs=out_specs, check_vma=False
    )
```

profile of v0, /device:TPU:0, one launch (start us, length us, event | category | flops | bytes accessed | tf_op | source)
XLA Modules:
  0.0 379.1 jit_solution(11920346828465409349)
XLA Ops:
  9.5 24.1 %all-gather.6.cloned.1.call-done = bf16[1024,512]{1,0:T(8,128)(2,1)} async-done(((bf16[512,512]{1,0:T(8,128)(2,1)}), bf16[1024,512]{1,0:T(8,128)(2,1)}) %all-gather.6.cloned.1.call-update) | async-done | bytes 1048592 | tf_op jit(solution)/shard_map/all_gather | solution.py:59
  33.6 1.8 fusion.44
  35.4 21.1 %all-gather.4.cloned.1.call-done = bf16[1024,512]{1,0:T(8,128)(2,1)} async-done(((bf16[512,512]{1,0:T(8,128)(2,1)}), bf16[1024,512]{1,0:T(8,128)(2,1)}) %all-gather.4.cloned.1.call-update) | async-done | bytes 1048592 | tf_op jit(solution)/shard_map/all_gather | solution.py:58
  56.5 1.8 fusion.43
  60.4 5.5 %collective-permute-start = (bf16[2,384,512]{2,1,0:T(8,128)(2,1)S(1)}, bf16[2,384,512]{2,1,0:T(8,128)(2,1)}, u32[]{:S(2)}, u32[]{:S(2)}) collective-permute-start(bf16[2,384,512]{2,1,0:T(8,128)(2,1)S(1)} %pad_maximum_fusion.1), channel_id=1, source_target_pairs={{0,4},{4,8},{8,12},{12,16},{16,20},{20,24},{24,28},{1,5},{5,9},{9,... | collective-permute-start | bytes 2359304 | tf_op jit(solution)/shard_map/ppermute | solution.py:19
  68.1 11.2 %all-gather.8.cloned.1.call-done = bf16[1024,512]{1,0:T(8,128)(2,1)} async-done(((bf16[512,512]{1,0:T(8,128)(2,1)}), bf16[1024,512]{1,0:T(8,128)(2,1)}) %all-gather.8.cloned.1.call-update) | async-done | bytes 1048592 | tf_op jit(solution)/shard_map/all_gather | solution.py:57
  79.4 1.8 convolution_convert_fusion.1
  82.9 14.1 %collective-permute-done = bf16[2,384,512]{2,1,0:T(8,128)(2,1)} collective-permute-done((bf16[2,384,512]{2,1,0:T(8,128)(2,1)S(1)}, bf16[2,384,512]{2,1,0:T(8,128)(2,1)}, u32[]{:S(2)}, u32[]{:S(2)}) %collective-permute-start) | collective-permute-done | bytes 786464 | tf_op jit(solution)/shard_map/ppermute | solution.py:19
  97.0 1.8 pad_maximum_fusion
  98.8 4.6 %reshape.200 = bf16[2,9,128,8,64]{4,3,2,1,0:T(8,128)(2,1)} reshape(bf16[2,1152,512]{2,1,0:T(8,128)(2,1)S(1)} %pad_maximum_fusion) | data formatting | bytes 4718592 | tf_op jit(solution)/shard_map/reshape | solution.py:67
  103.3 6.1 %copy.83 = bf16[2,9,128,8,64]{2,4,1,3,0:T(8,128)(2,1)} copy(bf16[2,9,128,8,64]{4,3,2,1,0:T(8,128)(2,1)} %reshape.200) | data formatting | bytes 4718592 | tf_op jit(solution)/shard_map/while | solution.py:96
  109.5 2.8 broadcast_in_dim.61
  112.3 76.9 %while.27 = (s32[]{:T(128)}, f32[2,9,128,8,64]{2,4,3,1,0:T(8,128)}, bf16[3,128,8,64]{1,3,2,0:T(8,128)(2,1)S(1)}, s32[3]{0:T(128)S(1)}, s32[3,7]{1,0:T(4,128)S(1)...) while((s32[]{:T(128)}, f32[2,9,128,8,64]{2,4,3,1,0:T(8,128)}, ...), condition=%wide.region_10.11_spmd, body=%wide.region_4.10_spmd.sunk | while | flops 611644544 | bytes 56669256 | solution.py:128
  116.2 2.1 select_reduce_fusion.5
  119.0 2.0 fusion.89
  121.1 2.6 multiply_reduce_fusion.2
  124.9 1.7 fusion.90
  128.9 4.8 %scatter_fusion = f32[2,9,128,8,64]{2,4,3,1,0:T(8,128)} fusion(f32[2,9,128,8,64]{2,4,3,1,0:T(8,128)} %get-tuple-element.398, s32[7]{0:T(128)S(1)} %select_bitcast_fusion.5, f32[7,128,8,64]{1,3,2,0:T(8,128)} %copy.129), kind=kCustom, calls=%fused_computation.clone.1 | custom fusion | flops 458752 | bytes 5505080 | tf_op jit(solution)/shard_map/while/body/eval_jaxpr/scatter-add | solution.py:124
  133.7 4.3 %scatter_fusion.1 = f32[2,9,128,8,64]{2,4,3,1,0:T(8,128)} fusion(f32[2,9,128,8,64]{2,4,3,1,0:T(8,128)} %scatter_fusion, s32[7]{0:T(128)S(1)} %get-tuple-element.349, f32[7,128,8,64]{1,3,2,0:T(8,128)S(1)} %copy.130), kind=kCustom, calls=%fused_computation.1.clone.1 | custom fusion | flops 458752 | bytes 5505080 | tf_op jit(solution)/shard_map/while/body/eval_jaxpr/scatter-add | solution.py:124
  141.9 2.1 select_reduce_fusion.5
  144.7 2.0 fusion.89
  146.8 2.6 multiply_reduce_fusion.2
  150.6 1.7 fusion.90
  154.6 4.8 %scatter_fusion = f32[2,9,128,8,64]{2,4,3,1,0:T(8,128)} fusion(f32[2,9,128,8,64]{2,4,3,1,0:T(8,128)} %get-tuple-element.398, s32[7]{0:T(128)S(1)} %select_bitcast_fusion.5, f32[7,128,8,64]{1,3,2,0:T(8,128)} %copy.129), kind=kCustom, calls=%fused_computation.clone.1 | custom fusion | flops 458752 | bytes 5505080 | tf_op jit(solution)/shard_map/while/body/eval_jaxpr/scatter-add | solution.py:124
  159.4 4.2 %scatter_fusion.1 = f32[2,9,128,8,64]{2,4,3,1,0:T(8,128)} fusion(f32[2,9,128,8,64]{2,4,3,1,0:T(8,128)} %scatter_fusion, s32[7]{0:T(128)S(1)} %get-tuple-element.349, f32[7,128,8,64]{1,3,2,0:T(8,128)S(1)} %copy.130), kind=kCustom, calls=%fused_computation.1.clone.1 | custom fusion | flops 458752 | bytes 5505080 | tf_op jit(solution)/shard_map/while/body/eval_jaxpr/scatter-add | solution.py:124
  167.5 2.1 select_reduce_fusion.5
  170.3 2.0 fusion.89
  172.4 2.6 multiply_reduce_fusion.2
  180.2 4.8 %scatter_fusion = f32[2,9,128,8,64]{2,4,3,1,0:T(8,128)} fusion(f32[2,9,128,8,64]{2,4,3,1,0:T(8,128)} %get-tuple-element.398, s32[7]{0:T(128)S(1)} %select_bitcast_fusion.5, f32[7,128,8,64]{1,3,2,0:T(8,128)} %copy.129), kind=kCustom, calls=%fused_computation.clone.1 | custom fusion | flops 458752 | bytes 5505080 | tf_op jit(solution)/shard_map/while/body/eval_jaxpr/scatter-add | solution.py:124
  185.0 4.2 %scatter_fusion.1 = f32[2,9,128,8,64]{2,4,3,1,0:T(8,128)} fusion(f32[2,9,128,8,64]{2,4,3,1,0:T(8,128)} %scatter_fusion, s32[7]{0:T(128)S(1)} %get-tuple-element.349, f32[7,128,8,64]{1,3,2,0:T(8,128)S(1)} %copy.130), kind=kCustom, calls=%fused_computation.1.clone.1 | custom fusion | flops 458752 | bytes 5505080 | tf_op jit(solution)/shard_map/while/body/eval_jaxpr/scatter-add | solution.py:124
  189.3 2.9 bitcast_convert_fusion
  192.3 5.4 %collective-permute-start.2 = (bf16[2,3,128,512]{2,3,1,0:T(8,128)(2,1)S(1)}, bf16[2,3,128,512]{2,3,1,0:T(8,128)(2,1)}, u32[]{:S(2)}, u32[]{:S(2)}) collective-permute-start(bf16[2,3,128,512]{2,3,1,0:T(8,128)(2,1)S(1)} %get-tuple-element.236), channel_id=1, source_target_pairs={{0,4},{4,8},{8,12},{12,16},{16,20},{20,24},{24,28},{1,5},{5,9},{9,... | collective-permute-start | bytes 2359304 | tf_op jit(solution)/shard_map/ppermute | solution.py:31
  201.6 29.0 %collective-permute-done.2 = bf16[2,3,128,512]{2,3,1,0:T(8,128)(2,1)} collective-permute-done((bf16[2,3,128,512]{2,3,1,0:T(8,128)(2,1)S(1)}, bf16[2,3,128,512]{2,3,1,0:T(8,128)(2,1)}, u32[]{:S(2)}, u32[]{:S(2)}) %collective-permute-start.2) | collective-permute-done | bytes 786464 | tf_op jit(solution)/shard_map/ppermute | solution.py:31
  230.7 2.1 fusion.41
  233.7 4.5 %convolution_convert_fusion = bf16[3,512,1024]{2,1,0:T(8,128)(2,1)} fusion(bf16[384,1,512]{0,2,1:T(8,128)(2,1)S(1)} %copy.97, bf16[384,1,512]{0,2,1:T(8,128)(2,1)S(1)} %copy.96, bf16[384,1,512]{0,2,1:T(8,128)(2,1)} %stack_reshape.3, bf16[1,384,1024]{2,1,0:T(8,128)(2,1)S(1)} %copy-done), kind=kOutput, calls=%fused_computation.64 | convolution fusion | flops 1210712064 | bytes 5111808 | tf_op jit(solution)/shard_map/tr,tcf->rcf/dot_general | solution.py:152
  238.1 4.7 %copy.120 = bf16[1024,1536]{1,0:T(8,128)(2,1)} copy(bf16[1024,1536]{0,1:T(8,128)(2,1)} %bitcast.204) | data formatting | bytes 6291456
  244.2 1.8 fusion.54
  246.0 71.7 %reduce-scatter.4.cloned.1.call-done = bf16[128,1536]{1,0:T(8,128)(2,1)} async-done(((bf16[1024,1536]{1,0:T(8,128)(2,1)}), bf16[128,1536]{1,0:T(8,128)(2,1)}) %reduce-scatter.4.cloned.1.call-update) | async-done | bytes 393232
  320.2 2.0 fusion.60
  324.0 27.1 %while.26 = (s32[]{:T(128)}, bf16[3,128,8,64]{1,3,2,0:T(8,128)(2,1)S(1)}, s32[3]{0:T(128)S(1)}, bf16[2,9,128,8,64]{2,4,1,3,0:T(8,128)(2,1)}, s32[3,7]{1,0:T(4,12...) while((s32[]{:T(128)}, ...), condition=%wide.region_3.4_spmd, body=%wide.region_0.3_spmd.sunk | while | flops 245954576 | bytes 13128970 | solution.py:96
  327.8 2.1 select_reduce_fusion.4
  330.6 2.4 fusion.82
  336.9 2.1 select_reduce_fusion.4
  339.7 2.4 fusion.82
  345.9 2.1 select_reduce_fusion.4
  348.7 2.4 fusion.82
  354.7 15.5 %all-reduce.7.cloned.1.call-done = bf16[1,384,1024]{2,1,0:T(8,128)(2,1)} async-done(((bf16[1,384,1024]{2,1,0:T(8,128)(2,1)}), bf16[1,384,1024]{2,1,0:T(8,128)(2,1)}) %all-reduce.7.cloned.1.call-update) | async-done | bytes 786448 | tf_op jit(solution)/shard_map/psum | solution.py:149
  370.2 2.1 copy.152
  (107 shorter events, 42.3 us)
Async XLA Ops:
  7.2 26.4 %copy-start = (bf16[1,384,1024]{2,1,0:T(8,128)(2,1)S(1)}, bf16[1,384,1024]{2,1,0:T(8,128)(2,1)}, u32[]{:S(2)}) copy-start(bf16[1,384,1024]{2,1,0:T(8,128)(2,1)} %param.18) | copy-start | bytes 2359300
  7.2 26.4 %all-gather.6.cloned.1.call-start = ((), (), s32[]{:S(2)}) async-start(), calls=%async_computation.2 | async-start | bytes 1572864 | tf_op jit(solution)/shard_map/all_gather | solution.py:59
  7.9 48.6 %all-gather.4.cloned.1.call-start = ((), (), s32[]{:S(2)}) async-start(), calls=%async_computation.1 | async-start | bytes 1572864 | tf_op jit(solution)/shard_map/all_gather | solution.py:58
  8.7 57.2 %copy-start.10 = (s32[24,7]{0,1:T(8,128)S(1)}, s32[24,7]{0,1:T(8,128)}, u32[]{:S(2)}) copy-start(s32[24,7]{0,1:T(8,128)} %param.22) | copy-start | bytes 2020
  8.7 57.3 %copy-start.9 = (bf16[1,384,512]{2,1,0:T(8,128)(2,1)S(1)}, bf16[1,384,512]{2,1,0:T(8,128)(2,1)}, u32[]{:S(2)}) copy-start(bf16[1,384,512]{2,1,0:T(8,128)(2,1)} %param.23) | copy-start | bytes 1179652
  8.7 70.7 %all-gather.8.cloned.1.call-start = ((), (), s32[]{:S(2)}) async-start(), calls=%async_computation.3 | async-start | bytes 1572864 | tf_op jit(solution)/shard_map/all_gather | solution.py:57
  9.4 308.3 %reduce-scatter.4.cloned.1.call-start = ((), (), s32[]{:S(2)}) async-start(), calls=%async_computation.5 | async-start | bytes 3538944
  35.4 30.5 %copy-start.4 = (bf16[1,384,512]{2,1,0:T(8,128)(2,1)}, bf16[1,384,512]{2,1,0:T(8,128)(2,1)S(1)}, u32[]{:S(2)}) copy-start(bf16[1,384,512]{2,1,0:T(8,128)(2,1)S(1)} %fusion.44) | copy-start | bytes 1179652
  58.3 0.7 copy-start.5
  59.1 22.9 %collective-permute-start.1 = (bf16[2,384,512]{2,1,0:T(8,128)(2,1)S(1)}, bf16[2,384,512]{2,1,0:T(8,128)(2,1)S(1)}, u32[]{:S(2)}, u32[]{:S(2)}) collective-permute-start(bf16[2,384,512]{2,1,0:T(8,128)(2,1)S(1)} %pad_maximum_fusion.1), channel_id=1, source_target_pairs={{4,0},{8,4},{12,8},{16,12},{20,16},{24,20},{28,24},{5,1},{9,5},{13... | collective-permute-start | bytes 2359304 | tf_op jit(solution)/shard_map/ppermute | solution.py:21
  60.4 36.6 %collective-permute-start = (bf16[2,384,512]{2,1,0:T(8,128)(2,1)S(1)}, bf16[2,384,512]{2,1,0:T(8,128)(2,1)}, u32[]{:S(2)}, u32[]{:S(2)}) collective-permute-start(bf16[2,384,512]{2,1,0:T(8,128)(2,1)S(1)} %pad_maximum_fusion.1), channel_id=1, source_target_pairs={{0,4},{4,8},{8,12},{12,16},{16,20},{20,24},{24,28},{1,5},{5,9},{9,... | collective-permute-start | bytes 2359304 | tf_op jit(solution)/shard_map/ppermute | solution.py:19
  82.1 0.9 copy-start.8
  109.5 2.9 copy-start.11
  189.3 3.1 copy-start.6
  192.3 38.3 %collective-permute-start.2 = (bf16[2,3,128,512]{2,3,1,0:T(8,128)(2,1)S(1)}, bf16[2,3,128,512]{2,3,1,0:T(8,128)(2,1)}, u32[]{:S(2)}, u32[]{:S(2)}) collective-permute-start(bf16[2,3,128,512]{2,3,1,0:T(8,128)(2,1)S(1)} %get-tuple-element.236), channel_id=1, source_target_pairs={{0,4},{4,8},{8,12},{12,16},{16,20},{20,24},{24,28},{1,5},{5,9},{9,... | collective-permute-start | bytes 2359304 | tf_op jit(solution)/shard_map/ppermute | solution.py:31
  197.7 33.0 %collective-permute-start.3 = (bf16[2,3,128,512]{2,3,1,0:T(8,128)(2,1)S(1)}, bf16[2,3,128,512]{2,3,1,0:T(8,128)(2,1)}, u32[]{:S(2)}, u32[]{:S(2)}) collective-permute-start(bf16[2,3,128,512]{2,3,1,0:T(8,128)(2,1)S(1)} %get-tuple-element.237), channel_id=1, source_target_pairs={{4,0},{8,4},{12,8},{16,12},{20,16},{24,20},{28,24},{5,1},{9,5},{13... | collective-permute-start | bytes 2359304 | tf_op jit(solution)/shard_map/ppermute | solution.py:31
  233.0 5.1 %copy-start.1 = (bf16[1,3,128,512]{3,2,1,0:T(8,128)(2,1)}, bf16[1,3,128,512]{3,2,1,0:T(8,128)(2,1)S(1)}, u32[]{:S(2)}) copy-start(bf16[1,3,128,512]{3,2,1,0:T(8,128)(2,1)S(1)} %copy.91) | copy-start | bytes 1179652
  233.2 4.9 %copy-start.2 = (bf16[1,3,128,512]{3,2,1,0:T(8,128)(2,1)}, bf16[1,3,128,512]{3,2,1,0:T(8,128)(2,1)S(1)}, u32[]{:S(2)}) copy-start(bf16[1,3,128,512]{3,2,1,0:T(8,128)(2,1)S(1)} %copy.92) | copy-start | bytes 1179652
  238.1 4.8 %copy-start.12 = (u32[32]{0:T(128)S(1)}, u32[32]{0:T(128)}, u32[]{:S(2)}) copy-start(u32[32]{0:T(128)} %constant.190) | copy-start | bytes 388
  242.9 109.8 %all-reduce.9.cloned.1.call-start = ((), (), s32[]{:S(2)}) async-start(), calls=%async_computation.6 | async-start | bytes 1048576
  246.0 76.2 %copy-start.3 = (bf16[1,3,128,512]{3,2,1,0:T(8,128)(2,1)S(1)}, bf16[1,3,128,512]{3,2,1,0:T(8,128)(2,1)}, u32[]{:S(2)}) copy-start(bf16[1,3,128,512]{3,2,1,0:T(8,128)(2,1)} %copy-done.2) | copy-start | bytes 1179652
  320.2 50.0 %all-reduce.7.cloned.1.call-start = ((), (), s32[]{:S(2)}) async-start(), calls=%async_computation.4 | async-start | bytes 1572864 | tf_op jit(solution)/shard_map/psum | solution.py:149
  320.2 2.1 copy-start.7
Sparse Core Ops, SparseCore 0:
  9.6 23.9 all-gather.5
  35.1 21.2 all-gather.3
  58.0 21.2 all-gather.7
  243.0 74.6 reduce-scatter.3
  320.3 27.6 all-reduce.8
  350.9 19.2 all-reduce.6
where the time goes:
time: 381 us; the launch traced here: 379 us
  waiting for transfers between devices  189 us (50%)
  matrix products  56 us (15%)
  other arithmetic  43.8 us (11%)
  local copies, waits for them, and re-layouts  41.8 us (11%)
  loops' own time  19.7 us (5%)
  between operations  15.1 us (4%)
  starting transfers between devices  13.9 us (4%)
    unnamed x8, waiting for transfers between devices  73.8 us
    ppermute x2, waiting for transfers between devices, shifted(): lax.ppermute(value, axis, [(source, source + steps) for source in range(l...  29 us
    scatter-add x6, other arithmetic, backward(): running.at[0, slot_rows].add(key_part).at[1, slot_rows].add(value_part)  27.2 us
    all_gather x1, waiting for transfers between devices, per_device(): lax.all_gather(w_value, 'dp', axis=0, tiled=True)  24.1 us
    all_gather x1, waiting for transfers between devices, per_device(): lax.all_gather(w_key, 'dp', axis=0, tiled=True)  21.1 us
    psum x1, waiting for transfers between devices, per_device(): grad_input = lax.psum(partial_input.astype(jnp.bfloat16), 'section')[None]  15.5 us
    ppermute x1, waiting for transfers between devices, extended(): lax.ppermute(tail, axis, [(i, (i + 1) % count) for i in range(ends)])  14.1 us
    unnamed x34, local copies, waits for them, and re-layouts  12.8 us
  transfers between devices with their start and end apart: 10, of which 7 were waited for; matrix products, arithmetic and copies ran while one was open for 10% of the time, Pallas kernels for 0%

commit v1 on v0

--- a/solution.py
+++ b/solution.py
@@ -6,6 +6,18 @@
 HD = 64
 BLOCK = 128
 REACH = 3
+
+
+def collect(array, axis, dim):
+    ways, here, turn = (lax.axis_size(axis), lax.axis_index(axis), array.shape[dim])
+    line, have = (array, 1)
+    while have < ways:
+        line = jnp.concatenate(
+            [line, lax.ppermute(line, axis, [(d, (d - have) % ways) for d in range(ways)])],
+            axis=dim,
+        )
+        have = 2 * have
+    return jnp.roll(line, here * turn, axis=dim)
 
 
 def extended(cells, sides, width):
@@ -56,7 +68,7 @@
     query_full, key_full, value_full = (
         lax.all_gather(w_query, "dp", axis=0, tiled=True),
         lax.all_gather(w_key, "dp", axis=0, tiled=True),
-        lax.all_gather(w_value, "dp", axis=0, tiled=True),
+        collect(w_value, "dp", 0),
     )
     queries = jnp.dot(tokens, query_full, preferred_element_type=jnp.float32).astype(jnp.bfloat16)
     key_rows = jnp.dot(tokens, key_full, preferred_element_type=jnp.float32).astype(jnp.bfloat16)

time: 381 us -> 361 us (0.948)
  waiting for transfers between devices: 189 us -> 160 us
    all_gather x1 -> x0, waiting for transfers between devices: 24.1 us -> none  [per_device(): lax.all_gather(w_value, 'dp', axis=0, tiled=True)]
    all_gather x1, waiting for transfers between devices: 21.1 us -> 3.79 us  [per_device(): lax.all_gather(w_key, 'dp', axis=0, tiled=True)]
    ppermute x0 -> x1, waiting for transfers between devices: none -> 14.8 us  [collect(): lax.ppermute(line, axis, [(d, (d - have) % ways) for d in range(ways)])]
    unnamed x34 -> x36, local copies, waits for them, and re-layouts: 12.8 us -> 13.8 us
    unnamed x8 -> x7, waiting for transfers between devices: 73.8 us -> 73.4 us
  transfers between devices with their start and end apart: 10 -> 10, of which waited for: 7 -> 7; matrix products, arithmetic and copies ran while one was open for 10% -> 12% of each run, Pallas kernels for 0% -> 0%
where the time goes in v1:
time: 361 us; the launch traced here: 359 us
  waiting for transfers between devices  160 us (44%)
  matrix products  55.5 us (15%)
  other arithmetic  47.3 us (13%)
  local copies, waits for them, and re-layouts  45.6 us (13%)
  loops' own time  19.7 us (5%)
  starting transfers between devices  16.6 us (5%)
  between operations  14.8 us (4%)
    unnamed x7, waiting for transfers between devices  73.4 us
    ppermute x2, waiting for transfers between devices, shifted(): lax.ppermute(value, axis, [(source, source + steps) for source in range(l...  29.2 us
    scatter-add x6, other arithmetic, backward(): running.at[0, slot_rows].add(key_part).at[1, slot_rows].add(value_part)  27.3 us
    psum x1, waiting for transfers between devices, per_device(): grad_input = lax.psum(partial_input.astype(jnp.bfloat16), 'section')[None]  15.5 us
    ppermute x1, waiting for transfers between devices, collect(): lax.ppermute(line, axis, [(d, (d - have) % ways) for d in range(ways)])  14.8 us
    unnamed x36, local copies, waits for them, and re-layouts  13.8 us
    dot_general x6, matrix products, attend(): jnp.einsum('qhd,skhd->hqsk', query_block, key_window, preferred_element_t...  12.4 us
    all_gather x1, waiting for transfers between devices, per_device(): lax.all_gather(w_query, 'dp', axis=0, tiled=True)  11.5 us
  transfers between devices with their start and end apart: 10, of which 7 were waited for; matrix products, arithmetic and copies ran while one was open for 12% of the time, Pallas kernels for 0%

profile of v1, /device:TPU:0, one launch (start us, length us, event | category | flops | bytes accessed | tf_op | source)
XLA Modules:
  0.0 359.0 jit_solution(8128511277250987157)
XLA Ops:
  8.0 3.0 collective-permute-start
  11.1 14.8 %collective-permute-done = bf16[512,512]{1,0:T(8,128)(2,1)S(1)} collective-permute-done((bf16[512,512]{1,0:T(8,128)(2,1)}, bf16[512,512]{1,0:T(8,128)(2,1)S(1)}, u32[]{:S(2)}, u32[]{:S(2)}) %collective-permute-start) | collective-permute-done | bytes 524320 | tf_op jit(solution)/shard_map/ppermute | solution.py:16
  25.9 3.4 fusion.52
  30.8 3.8 %all-gather.3.cloned.1.call-done = bf16[1024,512]{1,0:T(8,128)(2,1)} async-done(((bf16[512,512]{1,0:T(8,128)(2,1)}), bf16[1024,512]{1,0:T(8,128)(2,1)}) %all-gather.3.cloned.1.call-update) | async-done | bytes 1048592 | tf_op jit(solution)/shard_map/all_gather | solution.py:70
  34.6 1.8 fusion.43
  38.5 5.5 %collective-permute-start.1 = (bf16[2,384,512]{2,1,0:T(8,128)(2,1)S(1)}, bf16[2,384,512]{2,1,0:T(8,128)(2,1)}, u32[]{:S(2)}, u32[]{:S(2)}) collective-permute-start(bf16[2,384,512]{2,1,0:T(8,128)(2,1)S(1)} %pad_maximum_fusion.1), channel_id=1, source_target_pairs={{0,4},{4,8},{8,12},{12,16},{16,20},{20,24},{24,28},{1,5},{5,9},{9,... | collective-permute-start | bytes 2359304 | tf_op jit(solution)/shard_map/ppermute | solution.py:31
  47.5 11.5 %all-gather.5.cloned.1.call-done = bf16[1024,512]{1,0:T(8,128)(2,1)} async-done(((bf16[512,512]{1,0:T(8,128)(2,1)}), bf16[1024,512]{1,0:T(8,128)(2,1)}) %all-gather.5.cloned.1.call-update) | async-done | bytes 1048592 | tf_op jit(solution)/shard_map/all_gather | solution.py:69
  59.0 2.5 convolution_convert_fusion.2
  64.4 11.2 %collective-permute-done.1 = bf16[2,384,512]{2,1,0:T(8,128)(2,1)} collective-permute-done((bf16[2,384,512]{2,1,0:T(8,128)(2,1)S(1)}, bf16[2,384,512]{2,1,0:T(8,128)(2,1)}, u32[]{:S(2)}, u32[]{:S(2)}) %collective-permute-start.1) | collective-permute-done | bytes 786464 | tf_op jit(solution)/shard_map/ppermute | solution.py:31
  75.6 1.8 pad_maximum_fusion
  77.4 4.4 %reshape.200 = bf16[2,9,128,8,64]{4,3,2,1,0:T(8,128)(2,1)} reshape(bf16[2,1152,512]{2,1,0:T(8,128)(2,1)S(1)} %pad_maximum_fusion) | data formatting | bytes 4718592 | tf_op jit(solution)/shard_map/reshape | solution.py:79
  81.8 6.1 %copy.83 = bf16[2,9,128,8,64]{2,4,1,3,0:T(8,128)(2,1)} copy(bf16[2,9,128,8,64]{4,3,2,1,0:T(8,128)(2,1)} %reshape.200) | data formatting | bytes 4718592 | tf_op jit(solution)/shard_map/while | solution.py:108
  88.0 2.8 broadcast_in_dim.61
  90.8 77.0 %while.27 = (s32[]{:T(128)}, f32[2,9,128,8,64]{2,4,3,1,0:T(8,128)}, bf16[3,128,8,64]{1,3,2,0:T(8,128)(2,1)S(1)}, s32[3]{0:T(128)S(1)}, s32[3,7]{1,0:T(4,128)S(1)...) while((s32[]{:T(128)}, f32[2,9,128,8,64]{2,4,3,1,0:T(8,128)}, ...), condition=%wide.region_10.11_spmd, body=%wide.region_4.10_spmd.sunk | while | flops 611644544 | bytes 56669256 | solution.py:140
  94.7 2.1 select_reduce_fusion.5
  97.5 2.0 fusion.92
  99.6 2.6 multiply_reduce_fusion.2
  107.4 4.8 %scatter_fusion = f32[2,9,128,8,64]{2,4,3,1,0:T(8,128)} fusion(f32[2,9,128,8,64]{2,4,3,1,0:T(8,128)} %get-tuple-element.398, s32[7]{0:T(128)S(1)} %select_bitcast_fusion.5, f32[7,128,8,64]{1,3,2,0:T(8,128)} %copy.129), kind=kCustom, calls=%fused_computation.clone.1 | custom fusion | flops 458752 | bytes 5505080 | tf_op jit(solution)/shard_map/while/body/eval_jaxpr/scatter-add | solution.py:136
  112.2 4.3 %scatter_fusion.1 = f32[2,9,128,8,64]{2,4,3,1,0:T(8,128)} fusion(f32[2,9,128,8,64]{2,4,3,1,0:T(8,128)} %scatter_fusion, s32[7]{0:T(128)S(1)} %get-tuple-element.349, f32[7,128,8,64]{1,3,2,0:T(8,128)S(1)} %copy.130), kind=kCustom, calls=%fused_computation.1.clone.1 | custom fusion | flops 458752 | bytes 5505080 | tf_op jit(solution)/shard_map/while/body/eval_jaxpr/scatter-add | solution.py:136
  120.3 2.1 select_reduce_fusion.5
  123.1 2.0 fusion.92
  125.3 2.6 multiply_reduce_fusion.2
  129.0 1.7 fusion.93
  133.1 4.8 %scatter_fusion = f32[2,9,128,8,64]{2,4,3,1,0:T(8,128)} fusion(f32[2,9,128,8,64]{2,4,3,1,0:T(8,128)} %get-tuple-element.398, s32[7]{0:T(128)S(1)} %select_bitcast_fusion.5, f32[7,128,8,64]{1,3,2,0:T(8,128)} %copy.129), kind=kCustom, calls=%fused_computation.clone.1 | custom fusion | flops 458752 | bytes 5505080 | tf_op jit(solution)/shard_map/while/body/eval_jaxpr/scatter-add | solution.py:136
  137.9 4.3 %scatter_fusion.1 = f32[2,9,128,8,64]{2,4,3,1,0:T(8,128)} fusion(f32[2,9,128,8,64]{2,4,3,1,0:T(8,128)} %scatter_fusion, s32[7]{0:T(128)S(1)} %get-tuple-element.349, f32[7,128,8,64]{1,3,2,0:T(8,128)S(1)} %copy.130), kind=kCustom, calls=%fused_computation.1.clone.1 | custom fusion | flops 458752 | bytes 5505080 | tf_op jit(solution)/shard_map/while/body/eval_jaxpr/scatter-add | solution.py:136
  146.0 2.1 select_reduce_fusion.5
  148.8 2.0 fusion.92
  150.9 2.6 multiply_reduce_fusion.2
  158.7 4.8 %scatter_fusion = f32[2,9,128,8,64]{2,4,3,1,0:T(8,128)} fusion(f32[2,9,128,8,64]{2,4,3,1,0:T(8,128)} %get-tuple-element.398, s32[7]{0:T(128)S(1)} %select_bitcast_fusion.5, f32[7,128,8,64]{1,3,2,0:T(8,128)} %copy.129), kind=kCustom, calls=%fused_computation.clone.1 | custom fusion | flops 458752 | bytes 5505080 | tf_op jit(solution)/shard_map/while/body/eval_jaxpr/scatter-add | solution.py:136
  163.5 4.2 %scatter_fusion.1 = f32[2,9,128,8,64]{2,4,3,1,0:T(8,128)} fusion(f32[2,9,128,8,64]{2,4,3,1,0:T(8,128)} %scatter_fusion, s32[7]{0:T(128)S(1)} %get-tuple-element.349, f32[7,128,8,64]{1,3,2,0:T(8,128)S(1)} %copy.130), kind=kCustom, calls=%fused_computation.1.clone.1 | custom fusion | flops 458752 | bytes 5505080 | tf_op jit(solution)/shard_map/while/body/eval_jaxpr/scatter-add | solution.py:136
  167.8 2.9 bitcast_convert_fusion
  170.8 5.4 %collective-permute-start.3 = (bf16[2,3,128,512]{2,3,1,0:T(8,128)(2,1)S(1)}, bf16[2,3,128,512]{2,3,1,0:T(8,128)(2,1)}, u32[]{:S(2)}, u32[]{:S(2)}) collective-permute-start(bf16[2,3,128,512]{2,3,1,0:T(8,128)(2,1)S(1)} %get-tuple-element.236), channel_id=1, source_target_pairs={{0,4},{4,8},{8,12},{12,16},{16,20},{20,24},{24,28},{1,5},{5,9},{9,... | collective-permute-start | bytes 2359304 | tf_op jit(solution)/shard_map/ppermute | solution.py:43
  179.9 29.2 %collective-permute-done.3 = bf16[2,3,128,512]{2,3,1,0:T(8,128)(2,1)} collective-permute-done((bf16[2,3,128,512]{2,3,1,0:T(8,128)(2,1)S(1)}, bf16[2,3,128,512]{2,3,1,0:T(8,128)(2,1)}, u32[]{:S(2)}, u32[]{:S(2)}) %collective-permute-start.3) | collective-permute-done | bytes 786464 | tf_op jit(solution)/shard_map/ppermute | solution.py:43
  209.2 2.2 fusion.41
  212.9 4.4 %convolution_convert_fusion = bf16[3,512,1024]{2,1,0:T(8,128)(2,1)} fusion(bf16[384,1,512]{0,2,1:T(8,128)(2,1)S(1)} %copy.97, bf16[384,1,512]{0,2,1:T(8,128)(2,1)} %copy.96, bf16[384,1,512]{0,2,1:T(8,128)(2,1)S(1)} %copy-done.10, bf16[1,384,1024]{2,1,0:T(8,128)(2,1)S(1)} %copy-done), kind=kOutput, calls=%fused_computation.64 | convolution fusion | flops 1210712064 | bytes 5111808 | tf_op jit(solution)/shard_map/tr,tcf->rcf/dot_general | solution.py:164
  217.4 4.7 %copy.120 = bf16[1024,1536]{1,0:T(8,128)(2,1)} copy(bf16[1024,1536]{0,1:T(8,128)(2,1)} %bitcast.206) | data formatting | bytes 6291456
  223.5 1.8 fusion.57
  225.3 72.7 %reduce-scatter.4.cloned.1.call-done = bf16[128,1536]{1,0:T(8,128)(2,1)} async-done(((bf16[1024,1536]{1,0:T(8,128)(2,1)}), bf16[128,1536]{1,0:T(8,128)(2,1)}) %reduce-scatter.4.cloned.1.call-update) | async-done | bytes 393232
  300.5 2.0 fusion.63
  304.3 27.1 %while.26 = (s32[]{:T(128)}, bf16[3,128,8,64]{1,3,2,0:T(8,128)(2,1)S(1)}, s32[3]{0:T(128)S(1)}, bf16[2,9,128,8,64]{2,4,1,3,0:T(8,128)(2,1)}, s32[3,7]{1,0:T(4,12...) while((s32[]{:T(128)}, ...), condition=%wide.region_3.4_spmd, body=%wide.region_0.3_spmd.sunk | while | flops 245954576 | bytes 13128970 | solution.py:108
  308.1 2.1 select_reduce_fusion.4
  310.9 2.4 fusion.85
  317.1 2.1 select_reduce_fusion.4
  319.9 2.4 fusion.85
  326.2 2.1 select_reduce_fusion.4
  329.0 2.4 fusion.85
  334.9 15.5 %all-reduce.7.cloned.1.call-done = bf16[1,384,1024]{2,1,0:T(8,128)(2,1)} async-done(((bf16[1,384,1024]{2,1,0:T(8,128)(2,1)}), bf16[1,384,1024]{2,1,0:T(8,128)(2,1)}) %all-reduce.7.cloned.1.call-update) | async-done | bytes 786448 | tf_op jit(solution)/shard_map/psum | solution.py:161
  350.5 2.1 copy.152
  (109 shorter events, 46.9 us)
Async XLA Ops:
  7.2 23.0 %copy-start = (bf16[1,384,1024]{2,1,0:T(8,128)(2,1)S(1)}, bf16[1,384,1024]{2,1,0:T(8,128)(2,1)}, u32[]{:S(2)}) copy-start(bf16[1,384,1024]{2,1,0:T(8,128)(2,1)} %param.18) | copy-start | bytes 2359300
  7.2 27.4 %all-gather.3.cloned.1.call-start = ((), (), s32[]{:S(2)}) async-start(), calls=%async_computation.1 | async-start | bytes 1572864 | tf_op jit(solution)/shard_map/all_gather | solution.py:70
  7.9 51.0 %all-gather.5.cloned.1.call-start = ((), (), s32[]{:S(2)}) async-start(), calls=%async_computation.2 | async-start | bytes 1572864 | tf_op jit(solution)/shard_map/all_gather | solution.py:69
  8.0 17.9 %collective-permute-start = (bf16[512,512]{1,0:T(8,128)(2,1)}, bf16[512,512]{1,0:T(8,128)(2,1)S(1)}, u32[]{:S(2)}, u32[]{:S(2)}) collective-permute-start(bf16[512,512]{1,0:T(8,128)(2,1)} %param.21), channel_id=1, source_target_pairs={{0,2},{2,0},{1,3},{3,1},{4,6},{6,4},{5,7},{7,5},{8,10},{10,8},{9,1... | collective-permute-start | bytes 1572872 | tf_op jit(solution)/shard_map/ppermute | solution.py:16
  11.0 287.0 %reduce-scatter.4.cloned.1.call-start = ((), (), s32[]{:S(2)}) async-start(), calls=%async_computation.4 | async-start | bytes 3538944
  29.2 1.0 copy-start.1
  30.2 13.8 %copy-start.11 = (s32[24,7]{0,1:T(8,128)S(1)}, s32[24,7]{0,1:T(8,128)}, u32[]{:S(2)}) copy-start(s32[24,7]{0,1:T(8,128)} %param.22) | copy-start | bytes 2020
  30.8 30.7 %copy-start.6 = (bf16[1,384,512]{2,1,0:T(8,128)(2,1)}, bf16[1,384,512]{2,1,0:T(8,128)(2,1)S(1)}, u32[]{:S(2)}) copy-start(bf16[1,384,512]{2,1,0:T(8,128)(2,1)S(1)} %fusion.44) | copy-start | bytes 1179652
  36.4 0.7 copy-start.7
  37.2 26.3 %collective-permute-start.2 = (bf16[2,384,512]{2,1,0:T(8,128)(2,1)S(1)}, bf16[2,384,512]{2,1,0:T(8,128)(2,1)S(1)}, u32[]{:S(2)}, u32[]{:S(2)}) collective-permute-start(bf16[2,384,512]{2,1,0:T(8,128)(2,1)S(1)} %pad_maximum_fusion.1), channel_id=1, source_target_pairs={{4,0},{8,4},{12,8},{16,12},{20,16},{24,20},{28,24},{5,1},{9,5},{13... | collective-permute-start | bytes 2359304 | tf_op jit(solution)/shard_map/ppermute | solution.py:33
  38.5 37.1 %collective-permute-start.1 = (bf16[2,384,512]{2,1,0:T(8,128)(2,1)S(1)}, bf16[2,384,512]{2,1,0:T(8,128)(2,1)}, u32[]{:S(2)}, u32[]{:S(2)}) collective-permute-start(bf16[2,384,512]{2,1,0:T(8,128)(2,1)S(1)} %pad_maximum_fusion.1), channel_id=1, source_target_pairs={{0,4},{4,8},{8,12},{12,16},{16,20},{20,24},{24,28},{1,5},{5,9},{9,... | collective-permute-start | bytes 2359304 | tf_op jit(solution)/shard_map/ppermute | solution.py:31
  63.5 0.9 copy-start.9
  87.9 2.9 copy-start.12
  167.8 3.1 copy-start.8
  170.8 38.3 %collective-permute-start.3 = (bf16[2,3,128,512]{2,3,1,0:T(8,128)(2,1)S(1)}, bf16[2,3,128,512]{2,3,1,0:T(8,128)(2,1)}, u32[]{:S(2)}, u32[]{:S(2)}) collective-permute-start(bf16[2,3,128,512]{2,3,1,0:T(8,128)(2,1)S(1)} %get-tuple-element.236), channel_id=1, source_target_pairs={{0,4},{4,8},{8,12},{12,16},{16,20},{20,24},{24,28},{1,5},{5,9},{9,... | collective-permute-start | bytes 2359304 | tf_op jit(solution)/shard_map/ppermute | solution.py:43
  176.2 32.9 %collective-permute-start.4 = (bf16[2,3,128,512]{2,3,1,0:T(8,128)(2,1)S(1)}, bf16[2,3,128,512]{2,3,1,0:T(8,128)(2,1)}, u32[]{:S(2)}, u32[]{:S(2)}) collective-permute-start(bf16[2,3,128,512]{2,3,1,0:T(8,128)(2,1)S(1)} %get-tuple-element.237), channel_id=1, source_target_pairs={{4,0},{8,4},{12,8},{16,12},{20,16},{24,20},{28,24},{5,1},{9,5},{13... | collective-permute-start | bytes 2359304 | tf_op jit(solution)/shard_map/ppermute | solution.py:43
  209.2 3.8 %copy-start.10 = (bf16[384,1,512]{0,2,1:T(8,128)(2,1)S(1)}, bf16[384,1,512]{0,2,1:T(8,128)(2,1)}, u32[]{:S(2)}) copy-start(bf16[384,1,512]{0,2,1:T(8,128)(2,1)} %stack_reshape.3) | copy-start | bytes 1179652
  211.6 5.8 %copy-start.3 = (bf16[1,3,128,512]{3,2,1,0:T(8,128)(2,1)}, bf16[1,3,128,512]{3,2,1,0:T(8,128)(2,1)S(1)}, u32[]{:S(2)}) copy-start(bf16[1,3,128,512]{3,2,1,0:T(8,128)(2,1)S(1)} %copy.91) | copy-start | bytes 1179652
  211.8 5.6 %copy-start.4 = (bf16[1,3,128,512]{3,2,1,0:T(8,128)(2,1)}, bf16[1,3,128,512]{3,2,1,0:T(8,128)(2,1)S(1)}, u32[]{:S(2)}) copy-start(bf16[1,3,128,512]{3,2,1,0:T(8,128)(2,1)S(1)} %copy.92) | copy-start | bytes 1179652
  217.4 4.8 %copy-start.13 = (u32[32]{0:T(128)S(1)}, u32[32]{0:T(128)}, u32[]{:S(2)}) copy-start(u32[32]{0:T(128)} %constant.217) | copy-start | bytes 388
  222.1 110.9 %all-reduce.9.cloned.1.call-start = ((), (), s32[]{:S(2)}) async-start(), calls=%async_computation.5 | async-start | bytes 1048576
  225.3 77.3 %copy-start.5 = (bf16[1,3,128,512]{3,2,1,0:T(8,128)(2,1)S(1)}, bf16[1,3,128,512]{3,2,1,0:T(8,128)(2,1)}, u32[]{:S(2)}) copy-start(bf16[1,3,128,512]{3,2,1,0:T(8,128)(2,1)} %copy-done.4) | copy-start | bytes 1179652
  300.5 50.0 %all-reduce.7.cloned.1.call-start = ((), (), s32[]{:S(2)}) async-start(), calls=%async_computation.3 | async-start | bytes 1572864 | tf_op jit(solution)/shard_map/psum | solution.py:161
  300.5 2.1 copy-start.2
Sparse Core Ops, SparseCore 0:
  9.6 24.9 all-gather.2
  36.1 22.7 all-gather.4
  222.3 75.6 reduce-scatter.3
  300.6 27.6 all-reduce.8
  331.2 19.2 all-reduce.6
